TPU v7x, 256 devices: a whole 4x4x8 slice. The times are simulated.
256 devices in a mesh: gx: 8 (over y, core), gy: 8 (over z), ba: 4 (over x).
Axes of the slice: x: 4, y: 4, z: 8, core: 2. Of those that a mesh axis runs over, the one named last changes fastest.
Arguments:
- pixels: float32 [224, 128, 1024], P('ba', 'gy', 'gx'), may hold values from -8 to 8
- spectra: float32 [224, 256], P('ba'), may hold values from -0.375 to 0.375
- abundance: float32 [256, 128, 1024], P('ba', 'gy', 'gx'), may hold values from 0 to 1
- plan: int32 [3], replicated, may hold values from 0 to 1, as said below
Outputs:
- sparse: float32 [256, 128, 1024], P('ba', 'gy', 'gx')
- spectra_grad: float32 [224, 256], P('ba')
Inputs may be any that keep to these rules, and one draw needn't show every extreme that they name: `plan`: entry 0 is 1 and at least one later entry is 0.
All inputs are finite; a program needn't handle non-finite values. Where the computation divides by a largest or mean magnitude, that divisor is 1e-20 or more.
Results may differ from a plain program's by a relative error of at most 0.0001.
Values sent between devices are 32-bit elements; how exact they have to be, the bound alone decides.
No kernel may reach another device: no remote copies, remote signals or barrier semaphores. Data moves between devices by JAX's collectives and lax.ppermute only.
A program may use at most 64 MiB of HBM per device.

v0:
```python
import math

import jax
import jax.numpy as jnp
from jax import lax
from jax.sharding import PartitionSpec as P

SWEEPS = 3


HIGHEST = lax.Precision.HIGHEST
penalty = 1.0
tv_weight = 0.2
sparsity = 0.05


def extended_2(x, sides, width):
    for axis, dim in sides:
        size, length = (lax.axis_size(axis), x.shape[dim])
        up = [(i, (i + 1) % size) for i in range(size - 1)]
        down = [(j, i) for i, j in up]
        last = lax.slice_in_dim(x, length - width, length, axis=dim)
        leading = lax.slice_in_dim(x, 0, width, axis=dim)
        before = lax.ppermute(last, axis, up)
        after = lax.ppermute(leading, axis, down)
        x = jnp.concatenate([before, x, after], axis=dim)
    return x


def edge_masks(top_row, left_col, row_count, col_count, grid_rows, grid_cols):
    ext_rows = top_row - 1 + jnp.arange(row_count + 1)
    ext_cols = left_col - 1 + jnp.arange(col_count + 1)
    rows_in = (ext_rows >= 0) & (ext_rows <= grid_rows - 1)
    cols_in = (ext_cols >= 0) & (ext_cols <= grid_cols - 1)
    rows_ok = (ext_rows >= 0) & (ext_rows <= grid_rows - 2)
    cols_ok = (ext_cols >= 0) & (ext_cols <= grid_cols - 2)
    mask_h = (rows_in[:, None] & cols_ok[None, :]).astype(jnp.float32)[None]
    mask_v = (rows_ok[:, None] & cols_in[None, :]).astype(jnp.float32)[None]
    return (mask_h, mask_v)


def local(pixels, spectra, abundance, plan):
    comp_share, row_count, gx_cols = abundance.shape
    band_ways = lax.axis_size("ba")
    grid_rows = row_count * lax.axis_size("gy")
    grid_cols = gx_cols * lax.axis_size("gx")
    all_comps = comp_share * band_ways
    top_row = lax.axis_index("gy") * row_count
    all_spectra = lax.all_gather(spectra, "ba", axis=0, tiled=True)
    first_comp = lax.axis_index("ba") * comp_share
    own_cols = lax.dynamic_slice_in_dim(all_spectra, first_comp, comp_share, 1)
    gram_rows = jnp.dot(own_cols.T, all_spectra, precision=HIGHEST)
    bound = lax.pmax(jnp.max(jnp.sum(jnp.abs(gram_rows), axis=1)), "ba")
    left_col = lax.axis_index("gx") * gx_cols
    mask_h, mask_v = edge_masks(top_row, left_col, row_count, gx_cols, grid_rows, grid_cols)
    field = abundance
    sparse = abundance
    dual = jnp.zeros_like(abundance)
    weight = jnp.ones((comp_share, row_count + 1, gx_cols + 1), jnp.float32)
    for sweep in range(SWEEPS):
        extended = extended_2(field, (("gx", 2), ("gy", 1)), 1)
        center = extended[:, : row_count + 1, : gx_cols + 1]
        right = extended[:, : row_count + 1, 1:]
        below = extended[:, 1:, : gx_cols + 1]
        diff_h = (right - center) * mask_h
        diff_v = (below - center) * mask_v
        energy = diff_h * diff_h + diff_v * diff_v
        total = lax.psum(jnp.sum(energy[:, 1:, 1:]), ("gx", "gy", "ba"))
        smooth_sq = total / (all_comps * grid_rows * grid_cols) + 1e-06
        fresh = 1.0 / jnp.sqrt(energy + smooth_sq)
        weight = jnp.where(plan[sweep] == 1, fresh, weight)
        flux_h = weight * diff_h
        flux_v = weight * diff_v
        edge_h = weight * mask_h
        edge_v = weight * mask_v
        tv_grad = flux_h[:, 1:, :-1] - flux_h[:, 1:, 1:] + flux_v[:, :-1, 1:] - flux_v[:, 1:, 1:]
        degree = edge_h[:, 1:, 1:] + edge_h[:, 1:, :-1] + edge_v[:, 1:, 1:] + edge_v[:, :-1, 1:]
        mixed = jnp.einsum(
            "lq,qrc->lrc",
            spectra,
            lax.all_gather(field, "ba", axis=0, tiled=True),
            precision=HIGHEST,
        )
        resid = mixed - pixels
        data_grad = lax.psum_scatter(
            jnp.einsum("lp,lrc->prc", spectra, resid, precision=HIGHEST),
            "ba",
            scatter_dimension=0,
            tiled=True,
        )
        grad_total = data_grad + tv_weight * tv_grad + penalty * (field - sparse + dual)
        field = field - grad_total / (bound + penalty + 2.0 * tv_weight * degree)
        sparse = jnp.maximum(field + dual - sparsity / penalty, 0.0)
        dual = dual + field - sparse
    all_sparse = lax.all_gather(sparse, "ba", axis=0, tiled=True)
    resid = jnp.einsum("lp,prc->lrc", spectra, all_sparse, precision=HIGHEST) - pixels
    partial_grad = jnp.einsum("lrc,prc->lp", resid, all_sparse, precision=HIGHEST) / math.sqrt(
        grid_rows * grid_cols
    )
    spectra_grad = lax.psum(partial_grad, ("gx", "gy"))
    return (sparse, spectra_grad)


def solution(mesh):
    return jax.shard_map(
        local,
        mesh=mesh,
        in_specs=(P("ba", "gy", "gx"), P("ba", None), P("ba", "gy", "gx"), P()),
        out_specs=(P("ba", "gy", "gx"), P("ba", None)),
        check_vma=False,
    )
```

profile of v0, /device:TPU:2, one launch (start us, length us, event | category | flops | bytes accessed | tf_op | source)
XLA Modules:
  0.0 793.5 jit_solution(9205692723680209742)
XLA Ops:
  8.0 37.2 %all-gather.5.cloned.1.call-done = f32[256,16,128]{2,1,0:T(8,128)} async-done(((f32[64,16,128]{2,1,0:T(8,128)}), f32[256,16,128]{2,1,0:T(8,128)}) %all-gather.5.cloned.1.call-update) | async-done | bytes 2097168 | tf_op jit(solution)/shard_map/all_gather | solution.py:81
  45.1 3.5 fusion.4
  50.6 2.0 copy.19
  56.8 12.2 %all_gather.16 = f32[224,256]{1,0:T(8,128)S(1)} all-gather(f32[56,256]{1,0:T(8,128)S(1)} %copy-done.14), channel_id=1, replica_groups=mesh['gx'=8,'gy'=8,'ba'=4] {'ba'}, dimensions={0}, use_global_device_ids=true | all-gather | bytes 286720 | tf_op jit(solution)/shard_map/all_gather | solution.py:49
  70.8 3.5 collective-permute-start.2
  74.9 10.9 %pmax.7 = f32[]{:T(128)} all-reduce(f32[]{:T(128)} %reduce_max.9), channel_id=1, replica_groups=mesh['gx'=8,'gy'=8,'ba'=4] {'ba'}, use_global_device_ids=true, to_apply=%region_5.6 | all-reduce | flops 1 | bytes 8 | tf_op jit(solution)/shard_map/pmax | solution.py:53
  88.5 4.2 collective-permute-done.3
  96.1 78.7 %psum.28 = f32[]{:T(128)} all-reduce(f32[]{:T(128)} %slice_reduce_fusion.2), channel_id=1, replica_groups=mesh['gx'=8,'gy'=8,'ba'=4] {'gx','gy','ba'}, use_global_device_ids=true, to_apply=%region_2.0 | all-reduce | flops 1 | bytes 8 | tf_op jit(solution)/shard_map/psum | solution.py:68
  175.5 5.1 fusion.55
  180.6 6.1 fusion.45
  187.0 30.1 %all-gather.7.cloned.1.call-done = f32[256,16,128]{2,1,0:T(8,128)} async-done(((f32[64,16,128]{2,1,0:T(8,128)}), f32[256,16,128]{2,1,0:T(8,128)}) %all-gather.7.cloned.1.call-update) | async-done | bytes 2097168 | tf_op jit(solution)/shard_map/all_gather | solution.py:81
  217.1 3.5 fusion.2
  228.9 3.7 collective-permute-done.5
  233.1 3.5 collective-permute-start.6
  239.2 3.6 collective-permute-done.7
  246.3 83.2 %psum.29 = f32[]{:T(128)} all-reduce(f32[]{:T(128)} %slice_reduce_fusion.1), channel_id=1, replica_groups=mesh['gx'=8,'gy'=8,'ba'=4] {'gx','gy','ba'}, use_global_device_ids=true, to_apply=%region_8.9 | all-reduce | flops 1 | bytes 8 | tf_op jit(solution)/shard_map/psum | solution.py:68
  330.1 3.6 fusion.56
  334.9 2.7 fusion.68
  337.6 6.1 fusion.38
  344.0 29.8 %all-gather.9.cloned.1.call-done = f32[256,16,128]{2,1,0:T(8,128)} async-done(((f32[64,16,128]{2,1,0:T(8,128)}), f32[256,16,128]{2,1,0:T(8,128)}) %all-gather.9.cloned.1.call-update) | async-done | bytes 2097168 | tf_op jit(solution)/shard_map/all_gather | solution.py:81
  373.8 3.5 fusion
  385.6 3.7 collective-permute-done.9
  389.8 3.5 collective-permute-start.10
  395.9 3.6 collective-permute-done.11
  403.0 83.4 %psum.30 = f32[]{:T(128)} all-reduce(f32[]{:T(128)} %slice_reduce_fusion), channel_id=1, replica_groups=mesh['gx'=8,'gy'=8,'ba'=4] {'gx','gy','ba'}, use_global_device_ids=true, to_apply=%region_11.12 | all-reduce | flops 1 | bytes 8 | tf_op jit(solution)/shard_map/psum | solution.py:68
  487.1 3.7 fusion.57
  490.8 2.6 fusion.69
  493.4 6.1 fusion.49
  499.6 30.1 %all-gather.11.cloned.1.call-done = f32[256,16,128]{2,1,0:T(8,128)} async-done(((f32[64,16,128]{2,1,0:T(8,128)}), f32[256,16,128]{2,1,0:T(8,128)}) %all-gather.11.cloned.1.call-update) | async-done | bytes 2097168 | tf_op jit(solution)/shard_map/all_gather | solution.py:95
  529.7 3.7 fusion.6
  533.5 2.3 fusion.22
  535.8 250.9 %psum.31 = f32[56,256]{1,0:T(8,128)} all-reduce(f32[56,256]{1,0:T(8,128)S(1)} %fusion.22), channel_id=1, replica_groups=mesh['gx'=8,'gy'=8,'ba'=4] {'gx','gy'}, use_global_device_ids=true, to_apply=%region_12.13 | all-reduce | flops 14336 | bytes 114688 | tf_op jit(solution)/shard_map/psum | solution.py:100
  (96 shorter events, 44.2 us)
Async XLA Ops:
  7.2 41.5 %copy-start.10 = (f32[56,16,128]{2,1,0:T(8,128)S(1)}, f32[56,16,128]{2,1,0:T(8,128)}, u32[]{:S(2)}) copy-start(f32[56,16,128]{2,1,0:T(8,128)} %param.4) | copy-start | bytes 1376260
  7.2 38.0 %all-gather.5.cloned.1.call-start = ((), (), s32[]{:S(2)}) async-start(), calls=%async_computation.3 | async-start | bytes 2621440 | tf_op jit(solution)/shard_map/all_gather | solution.py:81
  7.9 40.9 %copy-start.14 = (f32[56,256]{1,0:T(8,128)S(1)}, f32[56,256]{1,0:T(8,128)}, u32[]{:S(2)}) copy-start(f32[56,256]{1,0:T(8,128)} %param.5) | copy-start | bytes 172036
  7.9 172.7 %reduce-scatter.4.cloned.1.call-start = ((), (), s32[]{:S(2)}) async-start(), calls=%async_computation.4 | async-start | bytes 2621440 | tf_op jit(solution)/shard_map/reduce_scatter | solution.py:85
  52.6 164.5 %all-gather.7.cloned.1.call-start = ((), (), s32[]{:S(2)}) async-start(), calls=%async_computation.5 | async-start | bytes 2621440 | tf_op jit(solution)/shard_map/all_gather | solution.py:81
  53.9 20.4 %copy-start.15 = (s32[3]{0:T(128)S(1)}, s32[3]{0:T(128)}, u32[]{:S(2)}) copy-start(s32[3]{0:T(128)} %param.7) | copy-start | bytes 40
  53.9 16.4 %collective-permute-start = (f32[64,16,1]{2,1,0:T(8,128)S(1)}, f32[64,16,1]{2,1,0:T(8,128)S(1)}, u32[]{:S(2)}, u32[]{:S(2)}) collective-permute-start(f32[64,16,1]{2,1,0:T(8,128)S(1)} %get-tuple-element.28), channel_id=1, source_target_pairs={{0,32},{32,64},{64,96},{96,128},{128,160},{160,192},{192,224},{1,3... | collective-permute-start | bytes 12296 | tf_op jit(solution)/shard_map/ppermute | solution.py:24
  55.5 14.8 %collective-permute-start.1 = (f32[64,16,1]{2,1,0:T(8,128)S(1)}, f32[64,16,1]{2,1,0:T(8,128)S(1)}, u32[]{:S(2)}, u32[]{:S(2)}) collective-permute-start(f32[64,16,1]{2,1,0:T(8,128)S(1)} %get-tuple-element.29), channel_id=1, source_target_pairs={{32,0},{64,32},{96,64},{128,96},{160,128},{192,160},{224,192},{33,... | collective-permute-start | bytes 12296 | tf_op jit(solution)/shard_map/ppermute | solution.py:25
  70.8 17.0 %collective-permute-start.2 = (f32[64,1,130]{2,1,0:T(1,128)S(1)}, f32[64,1,130]{2,1,0:T(1,128)S(1)}, u32[]{:S(2)}, u32[]{:S(2)}) collective-permute-start(f32[64,1,130]{2,1,0:T(1,128)S(1)} %get-tuple-element.23), channel_id=1, source_target_pairs={{0,4},{4,8},{8,12},{12,16},{16,20},{20,24},{24,28},{1,5},{5,9},{9,... | collective-permute-start | bytes 99848 | tf_op jit(solution)/shard_map/ppermute | solution.py:24
  86.5 6.2 collective-permute-start.3
  93.5 1.1 copy-start.3
  186.7 33.9 %copy-start.11 = (f32[56,16,128]{2,1,0:T(8,128)S(1)}, f32[56,16,128]{2,1,0:T(8,128)}, u32[]{:S(2)}) copy-start(f32[56,16,128]{2,1,0:T(8,128)} %param.4) | copy-start | bytes 1376260
  186.7 150.9 %reduce-scatter.6.cloned.1.call-start = ((), (), s32[]{:S(2)}) async-start(), calls=%async_computation.6 | async-start | bytes 2621440 | tf_op jit(solution)/shard_map/reduce_scatter | solution.py:85
  224.6 149.2 %all-gather.9.cloned.1.call-start = ((), (), s32[]{:S(2)}) async-start(), calls=%async_computation.7 | async-start | bytes 2621440 | tf_op jit(solution)/shard_map/all_gather | solution.py:81
  225.8 3.1 collective-permute-start.4
  227.4 5.2 collective-permute-start.5
  233.1 5.3 collective-permute-start.6
  236.6 6.2 collective-permute-start.7
  243.7 1.2 copy-start.6
  333.8 1.1 copy-start.4
  343.7 33.6 %copy-start.12 = (f32[56,16,128]{2,1,0:T(8,128)S(1)}, f32[56,16,128]{2,1,0:T(8,128)}, u32[]{:S(2)}) copy-start(f32[56,16,128]{2,1,0:T(8,128)} %param.4) | copy-start | bytes 1376260
  343.7 149.7 %reduce-scatter.8.cloned.1.call-start = ((), (), s32[]{:S(2)}) async-start(), calls=%async_computation.8 | async-start | bytes 2621440 | tf_op jit(solution)/shard_map/reduce_scatter | solution.py:85
  381.3 148.3 %all-gather.11.cloned.1.call-start = ((), (), s32[]{:S(2)}) async-start(), calls=%async_computation.9 | async-start | bytes 2621440 | tf_op jit(solution)/shard_map/all_gather | solution.py:95
  382.5 3.1 collective-permute-start.8
  384.1 5.2 collective-permute-start.9
  389.3 10.1 %copy-start.7 = (f32[64,16,1]{2,1,0:T(8,128)}, f32[64,16,1]{2,1,0:T(8,128)S(1)}, u32[]{:S(2)}) copy-start(f32[64,16,1]{2,1,0:T(8,128)S(1)} %collective-permute-done.9) | copy-start | bytes 12292
  389.8 5.3 collective-permute-start.10
  393.3 6.2 collective-permute-start.11
  400.4 1.2 copy-start.5
  487.1 3.7 copy-start.8
  499.6 33.8 %copy-start.13 = (f32[56,16,128]{2,1,0:T(8,128)S(1)}, f32[56,16,128]{2,1,0:T(8,128)}, u32[]{:S(2)}) copy-start(f32[56,16,128]{2,1,0:T(8,128)} %param.4) | copy-start | bytes 1376260
  529.6 3.8 copy-start.9
  (3 other events, 3.1 us)
Sparse Core Ops, SparseCore 0:
  9.8 35.2 all-gather.4
  52.8 32.7 reduce-scatter.3
  186.9 30.1 all-gather.6
  224.7 31.9 reduce-scatter.5
  343.9 29.8 all-gather.8
  381.4 31.9 reduce-scatter.7
  499.7 29.8 all-gather.10
where the time goes:
time: 795 us; the launch traced here: 794 us
  blocking collectives  519 us (65%)
  waiting for transfers between devices  148 us (19%)
  other arithmetic  46 us (6%)
  starting transfers between devices  23.6 us (3%)
  matrix products  22.7 us (3%)
  between operations  19.1 us (2%)
  local copies, waits for them, and re-layouts  14.7 us (2%)
    psum x1, blocking collectives, local(): spectra_grad = lax.psum(partial_grad, ('gx', 'gy'))  251 us
    psum x3, blocking collectives, local(): total = lax.psum(jnp.sum(energy[:, 1:, 1:]), ('gx', 'gy', 'ba'))  245 us
    all_gather x3, waiting for transfers between devices, local(): lax.all_gather(field, 'ba', axis=0, tiled=True)  97.1 us
    all_gather x1, waiting for transfers between devices, local(): all_sparse = lax.all_gather(sparse, 'ba', axis=0, tiled=True)  30.1 us
    ppermute x6, waiting for transfers between devices, extended_2(): after = lax.ppermute(leading, axis, down)  18.8 us
  transfers between devices with their start and end apart: 19, of which 13 were waited for; matrix products, arithmetic and copies ran while one was open for 4% of the time, Pallas kernels for 0%

commit v1 on v0

v1 whole, which is shorter than its diff:
```python
import math

import jax
import jax.numpy as jnp
from jax import lax
from jax.sharding import PartitionSpec as P

SWEEPS = 3


HIGHEST = lax.Precision.HIGHEST
penalty = 1.0
tv_weight = 0.2
sparsity = 0.05

ROWS = ("gy", "ba")


def extended_2(x, sides, width):
    for axis, size, dim in sides:
        length = x.shape[dim]
        up = [(i, i + 1) for i in range(size - 1)]
        down = [(j, i) for i, j in up]
        last = lax.slice_in_dim(x, length - width, length, axis=dim)
        leading = lax.slice_in_dim(x, 0, width, axis=dim)
        before = lax.ppermute(last, axis, up)
        after = lax.ppermute(leading, axis, down)
        x = jnp.concatenate([before, x, after], axis=dim)
    return x


def edge_masks(top_row, left_col, row_count, col_count, grid_rows, grid_cols):
    ext_rows = top_row - 1 + jnp.arange(row_count + 1)
    ext_cols = left_col - 1 + jnp.arange(col_count + 1)
    rows_in = (ext_rows >= 0) & (ext_rows <= grid_rows - 1)
    cols_in = (ext_cols >= 0) & (ext_cols <= grid_cols - 1)
    rows_ok = (ext_rows >= 0) & (ext_rows <= grid_rows - 2)
    cols_ok = (ext_cols >= 0) & (ext_cols <= grid_cols - 2)
    mask_h = (rows_in[:, None] & cols_ok[None, :]).astype(jnp.float32)[None]
    mask_v = (rows_ok[:, None] & cols_in[None, :]).astype(jnp.float32)[None]
    return (mask_h, mask_v)


def total_of(x, axes=("ba", "gy", "gx")):
    for axis in axes:
        x = lax.psum(x, axis)
    return x


def local(pixels, spectra, abundance, plan):
    band_ways = lax.axis_size("ba")
    row_ways = lax.axis_size("gy") * band_ways
    field = lax.all_to_all(abundance, "ba", 1, 0, tiled=True)
    bands = lax.all_to_all(pixels, "ba", 1, 0, tiled=True)
    all_comps, row_count, gx_cols = field.shape
    grid_rows = row_count * row_ways
    grid_cols = gx_cols * lax.axis_size("gx")
    row_block = lax.axis_index("gy") * band_ways + lax.axis_index("ba")
    top_row = row_block * row_count
    all_spectra = lax.all_gather(spectra, "ba", axis=0, tiled=True)
    gram = jnp.dot(all_spectra.T, all_spectra, precision=HIGHEST)
    bound = jnp.max(jnp.sum(jnp.abs(gram), axis=1))
    left_col = lax.axis_index("gx") * gx_cols
    mask_h, mask_v = edge_masks(top_row, left_col, row_count, gx_cols, grid_rows, grid_cols)
    sparse = field
    dual = jnp.zeros_like(field)
    weight = jnp.ones((all_comps, row_count + 1, gx_cols + 1), jnp.float32)
    for sweep in range(SWEEPS):
        extended = extended_2(field, (("gx", lax.axis_size("gx"), 2), (ROWS, row_ways, 1)), 1)
        center = extended[:, : row_count + 1, : gx_cols + 1]
        right = extended[:, : row_count + 1, 1:]
        below = extended[:, 1:, : gx_cols + 1]
        diff_h = (right - center) * mask_h
        diff_v = (below - center) * mask_v
        energy = diff_h * diff_h + diff_v * diff_v
        total = total_of(jnp.sum(energy[:, 1:, 1:]))
        smooth_sq = total / (all_comps * grid_rows * grid_cols) + 1e-06
        fresh = 1.0 / jnp.sqrt(energy + smooth_sq)
        weight = jnp.where(plan[sweep] == 1, fresh, weight)
        flux_h = weight * diff_h
        flux_v = weight * diff_v
        edge_h = weight * mask_h
        edge_v = weight * mask_v
        tv_grad = flux_h[:, 1:, :-1] - flux_h[:, 1:, 1:] + flux_v[:, :-1, 1:] - flux_v[:, 1:, 1:]
        degree = edge_h[:, 1:, 1:] + edge_h[:, 1:, :-1] + edge_v[:, 1:, 1:] + edge_v[:, :-1, 1:]
        resid = jnp.einsum("lq,qrc->lrc", all_spectra, field, precision=HIGHEST) - bands
        data_grad = jnp.einsum("lp,lrc->prc", all_spectra, resid, precision=HIGHEST)
        grad_total = data_grad + tv_weight * tv_grad + penalty * (field - sparse + dual)
        field = field - grad_total / (bound + penalty + 2.0 * tv_weight * degree)
        sparse = jnp.maximum(field + dual - sparsity / penalty, 0.0)
        dual = dual + field - sparse
    resid = jnp.einsum("lp,prc->lrc", all_spectra, sparse, precision=HIGHEST) - bands
    partial_grad = jnp.einsum("lrc,prc->lp", resid, sparse, precision=HIGHEST) / math.sqrt(
        grid_rows * grid_cols
    )
    spectra_grad = lax.psum_scatter(partial_grad, "ba", scatter_dimension=0, tiled=True)
    spectra_grad = total_of(spectra_grad, ("gx", "gy"))
    out = lax.all_to_all(sparse, "ba", 0, 1, tiled=True)
    return (out, spectra_grad)


def solution(mesh):
    return jax.shard_map(
        local,
        mesh=mesh,
        in_specs=(P("ba", "gy", "gx"), P("ba", None), P("ba", "gy", "gx"), P()),
        out_specs=(P("ba", "gy", "gx"), P("ba", None)),
        check_vma=False,
    )
```

time: 795 us -> 330 us (0.42)
  blocking collectives: 519 us -> 217 us
  waiting for transfers between devices: 148 us -> 26.4 us
  other arithmetic: 46 us -> 6.78 us
  starting transfers between devices: 23.6 us -> 39.2 us
  matrix products: 22.7 us -> 11.1 us
    psum x4 -> x11, blocking collectives: 496 us -> 190 us  [total_of(): x = lax.psum(x, axis)]
    all_gather x4 -> x0, waiting for transfers between devices: 127 us -> none  [the longest x3 97.1 us: local(): lax.all_gather(field, 'ba', axis=0, tiled=True)]
    all_to_all x0 -> x1, blocking collectives: none -> 14.7 us  [local(): out = lax.all_to_all(sparse, 'ba', 0, 1, tiled=True)]
    sub x6 -> x0, other arithmetic: 12.6 us -> none  [the longest x2 12.2 us: local(): field = field - grad_total / (bound + penalty + 2.0 * tv_weight * degree)]
    dot_general x9, matrix products: 22.7 us -> 11.1 us  [the longest x3 4.26 us: local(): data_grad = jnp.einsum('lp,lrc->prc', all_spectra, resid, precision=HIGHEST)]
    all_to_all x0 -> x2, starting transfers between devices: none -> 11.3 us  [the longest x1 5.81 us: local(): field = lax.all_to_all(abundance, 'ba', 1, 0, tiled=True)]
    pmax x1 -> x0, blocking collectives: 10.9 us -> none  [local(): bound = lax.pmax(jnp.max(jnp.sum(jnp.abs(gram_rows), axis=1)), 'ba')]
    mul x3, other arithmetic: 12.5 us -> 2.02 us  [local(): flux_h = weight * diff_h]
  transfers between devices with their start and end apart: 19 -> 15, of which waited for: 13 -> 9; matrix products, arithmetic and copies ran while one was open for 4% -> 2% of each run, Pallas kernels for 0% -> 0%
where the time goes in v1:
time: 330 us; the launch traced here: 329 us
  blocking collectives  217 us (66%)
  starting transfers between devices  39.2 us (12%)
  waiting for transfers between devices  26.4 us (8%)
  between operations  18.8 us (6%)
  matrix products  11.1 us (3%)
  local copies, waits for them, and re-layouts  9.42 us (3%)
  other arithmetic  6.78 us (2%)
    psum x11, blocking collectives, total_of(): x = lax.psum(x, axis)  190 us
    ppermute x6, starting transfers between devices, extended_2(): before = lax.ppermute(last, axis, up)  15.3 us
    all_to_all x1, blocking collectives, local(): out = lax.all_to_all(sparse, 'ba', 0, 1, tiled=True)  14.7 us
    ppermute x6, waiting for transfers between devices, extended_2(): after = lax.ppermute(leading, axis, down)  13.5 us
    ppermute x6, starting transfers between devices, extended_2(): after = lax.ppermute(leading, axis, down)  12.6 us
    all_gather x1, blocking collectives, local(): all_spectra = lax.all_gather(spectra, 'ba', axis=0, tiled=True)  12.3 us
    unnamed x21, local copies, waits for them, and re-layouts  7.19 us
  transfers between devices with their start and end apart: 15, of which 9 were waited for; matrix products, arithmetic and copies ran while one was open for 2% of the time, Pallas kernels for 0%

profile of v1, /device:TPU:2, one launch (start us, length us, event | category | flops | bytes accessed | tf_op | source)
XLA Modules:
  0.0 328.7 jit_solution(17367506952207164273)
XLA Ops:
  7.2 2.0 copy.35
  9.2 5.8 %all-to-all-start = ((f32[64,16,128]{2,0,1:T(8,128)}), f32[64,16,128]{2,0,1:T(8,128)S(1)}, u32[]{:S(2)}, u32[]{:S(2)}) async-start(f32[64,16,128]{2,0,1:T(8,128)} %copy.35), calls=%async_computation | async-start | bytes 1048576 | tf_op jit(solution)/shard_map/all_to_all | solution.py:53
  16.1 6.1 %all-to-all-done = f32[64,16,128]{2,0,1:T(8,128)S(1)} async-done(((f32[64,16,128]{2,0,1:T(8,128)}), f32[64,16,128]{2,0,1:T(8,128)S(1)}, u32[]{:S(2)}, u32[]{:S(2)}) %all-to-all-start) | async-done | bytes 524320 | tf_op jit(solution)/shard_map/all_to_all | solution.py:53
  22.1 5.5 %all-to-all-start.1 = ((f32[56,16,128]{2,0,1:T(8,128)}), f32[56,16,128]{2,0,1:T(8,128)}, u32[]{:S(2)}, u32[]{:S(2)}) async-start(f32[56,16,128]{2,0,1:T(8,128)} %copy.37), calls=%async_computation.1 | async-start | bytes 917504 | tf_op jit(solution)/shard_map/all_to_all | solution.py:54
  30.6 12.3 %all_gather.3 = f32[224,256]{1,0:T(8,128)S(1)} all-gather(f32[56,256]{1,0:T(8,128)S(1)} %copy-done.7), channel_id=1, replica_groups=mesh['gx'=8,'gy'=8,'ba'=4] {'ba'}, dimensions={0}, use_global_device_ids=true | all-gather | bytes 286720 | tf_op jit(solution)/shard_map/all_gather | solution.py:60
  42.9 2.2 collective-permute-start.2
  45.8 3.7 %collective-permute-start.3 = (f32[256,1,130]{0,2,1:T(8,128)S(1)}, f32[256,1,130]{0,2,1:T(8,128)S(1)}, u32[]{:S(2)}, u32[]{:S(2)}) collective-permute-start(f32[256,1,130]{0,2,1:T(8,128)S(1)} %get-tuple-element.24), channel_id=1, source_target_pairs={{1,0},{2,1},{3,2},{4,3},{5,4},{6,5},{7,6},{8,7},{9,8},{10,9},{11,1... | collective-permute-start | bytes 399368 | tf_op jit(solution)/shard_map/ppermute | solution.py:27
  51.4 2.3 collective-permute-done.3
  55.4 11.8 %psum.77 = f32[]{:T(128)} all-reduce(f32[]{:T(128)} %slice_reduce_fusion.2), channel_id=1, replica_groups=mesh['gx'=8,'gy'=8,'ba'=4] {'ba'}, use_global_device_ids=true, to_apply=%region_1.0 | all-reduce | flops 1 | bytes 8 | tf_op jit(solution)/shard_map/psum | solution.py:46
  68.3 19.7 %psum.78 = f32[]{:T(128)} all-reduce(f32[]{:T(128)} %psum.77), channel_id=1, replica_groups=mesh['gx'=8,'gy'=8,'ba'=4] {'gy'}, use_global_device_ids=true, to_apply=%region_2.0 | all-reduce | flops 1 | bytes 8 | tf_op jit(solution)/shard_map/psum | solution.py:46
  89.4 15.5 %psum.79 = f32[]{:T(128)} all-reduce(f32[]{:T(128)} %psum.78), channel_id=1, replica_groups=mesh['gx'=8,'gy'=8,'ba'=4] {'gx'}, use_global_device_ids=true, to_apply=%region_3.0 | all-reduce | flops 1 | bytes 8 | tf_op jit(solution)/shard_map/psum | solution.py:46
  107.9 2.2 collective-permute-start.4
  111.5 1.8 collective-permute-done.5
  113.2 3.9 %collective-permute-start.6 = (f32[256,1,130]{0,2,1:T(8,128)S(1)}, f32[256,1,130]{0,2,1:T(8,128)S(1)}, u32[]{:S(2)}, u32[]{:S(2)}) collective-permute-start(f32[256,1,130]{0,2,1:T(8,128)S(1)} %get-tuple-element.23), channel_id=1, source_target_pairs={{0,1},{1,2},{2,3},{3,4},{4,5},{5,6},{6,7},{7,8},{8,9},{9,10},{10,1... | collective-permute-start | bytes 399368 | tf_op jit(solution)/shard_map/ppermute | solution.py:26
  117.2 2.5 collective-permute-start.7
  121.1 3.8 %collective-permute-done.7 = f32[256,1,130]{0,2,1:T(8,128)S(1)} collective-permute-done((f32[256,1,130]{0,2,1:T(8,128)S(1)}, f32[256,1,130]{0,2,1:T(8,128)S(1)}, u32[]{:S(2)}, u32[]{:S(2)}) %collective-permute-start.7) | collective-permute-done | bytes 133152 | tf_op jit(solution)/shard_map/ppermute | solution.py:27
  126.0 10.9 %psum.80 = f32[]{:T(128)} all-reduce(f32[]{:T(128)} %slice_reduce_fusion.1), channel_id=1, replica_groups=mesh['gx'=8,'gy'=8,'ba'=4] {'ba'}, use_global_device_ids=true, to_apply=%region_7.8 | all-reduce | flops 1 | bytes 8 | tf_op jit(solution)/shard_map/psum | solution.py:46
  137.6 19.4 %psum.81 = f32[]{:T(128)} all-reduce(f32[]{:T(128)} %psum.80), channel_id=1, replica_groups=mesh['gx'=8,'gy'=8,'ba'=4] {'gy'}, use_global_device_ids=true, to_apply=%region_8.9 | all-reduce | flops 1 | bytes 8 | tf_op jit(solution)/shard_map/psum | solution.py:46
  158.4 13.0 %psum.82 = f32[]{:T(128)} all-reduce(f32[]{:T(128)} %psum.81), channel_id=1, replica_groups=mesh['gx'=8,'gy'=8,'ba'=4] {'gx'}, use_global_device_ids=true, to_apply=%region_9.10 | all-reduce | flops 1 | bytes 8 | tf_op jit(solution)/shard_map/psum | solution.py:46
  175.1 1.8 collective-permute-start.8
  178.2 1.8 collective-permute-done.9
  180.0 3.9 %collective-permute-start.10 = (f32[256,1,130]{0,2,1:T(8,128)S(1)}, f32[256,1,130]{0,2,1:T(8,128)S(1)}, u32[]{:S(2)}, u32[]{:S(2)}) collective-permute-start(f32[256,1,130]{0,2,1:T(8,128)S(1)} %get-tuple-element.21), channel_id=1, source_target_pairs={{0,1},{1,2},{2,3},{3,4},{4,5},{5,6},{6,7},{7,8},{8,9},{9,10},{10,1... | collective-permute-start | bytes 399368 | tf_op jit(solution)/shard_map/ppermute | solution.py:26
  183.9 2.5 collective-permute-start.11
  187.9 3.8 %collective-permute-done.11 = f32[256,1,130]{0,2,1:T(8,128)S(1)} collective-permute-done((f32[256,1,130]{0,2,1:T(8,128)S(1)}, f32[256,1,130]{0,2,1:T(8,128)S(1)}, u32[]{:S(2)}, u32[]{:S(2)}) %collective-permute-start.11) | collective-permute-done | bytes 133152 | tf_op jit(solution)/shard_map/ppermute | solution.py:27
  193.6 10.8 %psum.83 = f32[]{:T(128)} all-reduce(f32[]{:T(128)} %slice_reduce_fusion), channel_id=1, replica_groups=mesh['gx'=8,'gy'=8,'ba'=4] {'ba'}, use_global_device_ids=true, to_apply=%region_11.12 | all-reduce | flops 1 | bytes 8 | tf_op jit(solution)/shard_map/psum | solution.py:46
  205.0 19.5 %psum.84 = f32[]{:T(128)} all-reduce(f32[]{:T(128)} %psum.83), channel_id=1, replica_groups=mesh['gx'=8,'gy'=8,'ba'=4] {'gy'}, use_global_device_ids=true, to_apply=%region_12.13 | all-reduce | flops 1 | bytes 8 | tf_op jit(solution)/shard_map/psum | solution.py:46
  226.0 13.2 %psum.85 = f32[]{:T(128)} all-reduce(f32[]{:T(128)} %psum.84), channel_id=1, replica_groups=mesh['gx'=8,'gy'=8,'ba'=4] {'gx'}, use_global_device_ids=true, to_apply=%region_13.14 | all-reduce | flops 1 | bytes 8 | tf_op jit(solution)/shard_map/psum | solution.py:46
  242.2 1.5 fusion.14
  245.9 14.7 %all_to_all.54 = f32[256,4,128]{2,1,0:T(4,128)S(1)} all-to-all(f32[256,4,128]{2,1,0:T(4,128)S(1)} %copy.47), channel_id=1, replica_groups=mesh['gx'=8,'gy'=8,'ba'=4] {'ba'}, dimensions={0} | all-to-all | bytes 1048576 | tf_op jit(solution)/shard_map/all_to_all | solution.py:98
  261.8 4.1 %reduce-scatter.2.cloned.1.call-done = f32[56,256]{1,0:T(8,128)} async-done(((f32[224,256]{1,0:T(8,128)}), f32[56,256]{1,0:T(8,128)}) %reduce-scatter.2.cloned.1.call-update) | async-done | bytes 57360 | tf_op jit(solution)/shard_map/reduce_scatter | solution.py:96
  265.9 24.7 %psum.86 = f32[56,256]{1,0:T(8,128)S(1)} all-reduce(f32[56,256]{1,0:T(8,128)} %reduce-scatter.2.cloned.1.call-done), channel_id=1, replica_groups=mesh['gx'=8,'gy'=8,'ba'=4] {'gx'}, use_global_device_ids=true, to_apply=%region_15.16 | all-reduce | flops 14336 | bytes 114688 | tf_op jit(solution)/shard_map/psum | solution.py:46
  290.6 31.3 %psum.87 = f32[56,256]{1,0:T(8,128)} all-reduce(f32[56,256]{1,0:T(8,128)S(1)} %psum.86), channel_id=1, replica_groups=mesh['gx'=8,'gy'=8,'ba'=4] {'gy'}, use_global_device_ids=true, to_apply=%region_16.17 | all-reduce | flops 14336 | bytes 114688 | tf_op jit(solution)/shard_map/psum | solution.py:46
  (74 shorter events, 31.7 us)
Async XLA Ops:
  9.2 5.8 %copy-start.3 = (f32[56,16,128]{2,1,0:T(8,128)S(1)}, f32[56,16,128]{2,1,0:T(8,128)}, u32[]{:S(2)}) copy-start(f32[56,16,128]{2,1,0:T(8,128)} %param.4) | copy-start | bytes 1376260
  9.2 13.0 %all-to-all-start = ((f32[64,16,128]{2,0,1:T(8,128)}), f32[64,16,128]{2,0,1:T(8,128)S(1)}, u32[]{:S(2)}, u32[]{:S(2)}) async-start(f32[64,16,128]{2,0,1:T(8,128)} %copy.35), calls=%async_computation | async-start | bytes 1048576 | tf_op jit(solution)/shard_map/all_to_all | solution.py:53
  22.1 45.1 %all-to-all-start.1 = ((f32[56,16,128]{2,0,1:T(8,128)}), f32[56,16,128]{2,0,1:T(8,128)}, u32[]{:S(2)}, u32[]{:S(2)}) async-start(f32[56,16,128]{2,0,1:T(8,128)} %copy.37), calls=%async_computation.1 | async-start | bytes 917504 | tf_op jit(solution)/shard_map/all_to_all | solution.py:54
  27.7 238.2 %reduce-scatter.2.cloned.1.call-start = ((), (), s32[]{:S(2)}) async-start(), calls=%async_computation.4 | async-start | bytes 286720 | tf_op jit(solution)/shard_map/reduce_scatter | solution.py:96
  27.7 2.8 copy-start.7
  28.0 14.9 %collective-permute-start = (f32[256,4,1]{0,2,1:T(1,128)S(1)}, f32[256,4,1]{0,2,1:T(1,128)S(1)}, u32[]{:S(2)}, u32[]{:S(2)}) collective-permute-start(f32[256,4,1]{0,2,1:T(1,128)S(1)} %get-tuple-element.30), channel_id=1, source_target_pairs={{0,32},{32,64},{64,96},{96,128},{128,160},{160,192},{192,224},{1,3... | collective-permute-start | bytes 12296 | tf_op jit(solution)/shard_map/ppermute | solution.py:26
  29.3 13.6 %collective-permute-start.1 = (f32[256,4,1]{0,2,1:T(1,128)S(1)}, f32[256,4,1]{0,2,1:T(1,128)S(1)}, u32[]{:S(2)}, u32[]{:S(2)}) collective-permute-start(f32[256,4,1]{0,2,1:T(1,128)S(1)} %get-tuple-element.31), channel_id=1, source_target_pairs={{32,0},{64,32},{96,64},{128,96},{160,128},{192,160},{224,192},{33,... | collective-permute-start | bytes 12296 | tf_op jit(solution)/shard_map/ppermute | solution.py:27
  42.9 8.4 %collective-permute-start.2 = (f32[256,1,130]{0,2,1:T(8,128)S(1)}, f32[256,1,130]{0,2,1:T(8,128)S(1)}, u32[]{:S(2)}, u32[]{:S(2)}) collective-permute-start(f32[256,1,130]{0,2,1:T(8,128)S(1)} %get-tuple-element.25), channel_id=1, source_target_pairs={{0,1},{1,2},{2,3},{3,4},{4,5},{5,6},{6,7},{7,8},{8,9},{9,10},{10,1... | collective-permute-start | bytes 399368 | tf_op jit(solution)/shard_map/ppermute | solution.py:26
  45.7 3.7 %copy-start.8 = (s32[3]{0:T(128)S(1)}, s32[3]{0:T(128)}, u32[]{:S(2)}) copy-start(s32[3]{0:T(128)} %param.7) | copy-start | bytes 40
  45.8 8.0 %collective-permute-start.3 = (f32[256,1,130]{0,2,1:T(8,128)S(1)}, f32[256,1,130]{0,2,1:T(8,128)S(1)}, u32[]{:S(2)}, u32[]{:S(2)}) collective-permute-start(f32[256,1,130]{0,2,1:T(8,128)S(1)} %get-tuple-element.24), channel_id=1, source_target_pairs={{1,0},{2,1},{3,2},{4,3},{5,4},{6,5},{7,6},{8,7},{9,8},{10,9},{11,1... | collective-permute-start | bytes 399368 | tf_op jit(solution)/shard_map/ppermute | solution.py:27
  105.5 1.0 copy-start.6
  107.9 3.6 %collective-permute-start.4 = (f32[256,4,1]{0,2,1:T(1,128)S(1)}, f32[256,4,1]{0,2,1:T(1,128)S(1)}, u32[]{:S(2)}, u32[]{:S(2)}) collective-permute-start(f32[256,4,1]{0,2,1:T(1,128)S(1)} %get-tuple-element.28), channel_id=1, source_target_pairs={{0,32},{32,64},{64,96},{96,128},{128,160},{160,192},{192,224},{1,3... | collective-permute-start | bytes 12296 | tf_op jit(solution)/shard_map/ppermute | solution.py:26
  110.2 3.1 collective-permute-start.5
  113.2 7.8 %collective-permute-start.6 = (f32[256,1,130]{0,2,1:T(8,128)S(1)}, f32[256,1,130]{0,2,1:T(8,128)S(1)}, u32[]{:S(2)}, u32[]{:S(2)}) collective-permute-start(f32[256,1,130]{0,2,1:T(8,128)S(1)} %get-tuple-element.23), channel_id=1, source_target_pairs={{0,1},{1,2},{2,3},{3,4},{4,5},{5,6},{6,7},{7,8},{8,9},{9,10},{10,1... | collective-permute-start | bytes 399368 | tf_op jit(solution)/shard_map/ppermute | solution.py:26
  117.2 7.8 %collective-permute-start.7 = (f32[256,1,130]{0,2,1:T(8,128)S(1)}, f32[256,1,130]{0,2,1:T(8,128)S(1)}, u32[]{:S(2)}, u32[]{:S(2)}) collective-permute-start(f32[256,1,130]{0,2,1:T(8,128)S(1)} %get-tuple-element.22), channel_id=1, source_target_pairs={{1,0},{2,1},{3,2},{4,3},{5,4},{6,5},{7,6},{8,7},{9,8},{10,9},{11,1... | collective-permute-start | bytes 399368 | tf_op jit(solution)/shard_map/ppermute | solution.py:27
  172.4 0.9 copy-start
  172.4 1.3 copy-start.5
  175.1 3.1 collective-permute-start.8
  176.9 3.1 collective-permute-start.9
  180.0 7.8 %collective-permute-start.10 = (f32[256,1,130]{0,2,1:T(8,128)S(1)}, f32[256,1,130]{0,2,1:T(8,128)S(1)}, u32[]{:S(2)}, u32[]{:S(2)}) collective-permute-start(f32[256,1,130]{0,2,1:T(8,128)S(1)} %get-tuple-element.21), channel_id=1, source_target_pairs={{0,1},{1,2},{2,3},{3,4},{4,5},{5,6},{6,7},{7,8},{8,9},{9,10},{10,1... | collective-permute-start | bytes 399368 | tf_op jit(solution)/shard_map/ppermute | solution.py:26
  183.9 7.8 %collective-permute-start.11 = (f32[256,1,130]{0,2,1:T(8,128)S(1)}, f32[256,1,130]{0,2,1:T(8,128)S(1)}, u32[]{:S(2)}, u32[]{:S(2)}) collective-permute-start(f32[256,1,130]{0,2,1:T(8,128)S(1)} %get-tuple-element.20), channel_id=1, source_target_pairs={{1,0},{2,1},{3,2},{4,3},{5,4},{6,5},{7,6},{8,7},{9,8},{10,9},{11,1... | collective-permute-start | bytes 399368 | tf_op jit(solution)/shard_map/ppermute | solution.py:27
  192.1 0.9 copy-start.2
  224.5 15.3 %copy-start.1 = (f32[256,5,129]{0,2,1:T(8,128)S(1)}, f32[256,5,129]{0,2,1:T(8,128)}, u32[]{:S(2)}) copy-start(f32[256,5,129]{0,2,1:T(8,128)} %copy-done) | copy-start | bytes 1981444
  241.2 1.0 copy-start.4
Sparse Core Ops, SparseCore 0:
  245.8 20.0 reduce-scatter.1

commit v2 on v1

--- a/solution.py
+++ b/solution.py
@@ -43,7 +43,11 @@
 
 def total_of(x, axes=("ba", "gy", "gx")):
     for axis in axes:
-        x = lax.psum(x, axis)
+        size = lax.axis_size(axis)
+        step = 1
+        while step < size:
+            x = x + lax.ppermute(x, axis, [(i, i ^ step) for i in range(size)])
+            step *= 2
     return x
 
 

time: 330 us -> 299 us (0.906)
  blocking collectives: 217 us -> 13.8 us
  starting transfers between devices: 39.2 us -> 146 us
  waiting for transfers between devices: 26.4 us -> 74.7 us
  between operations: 18.8 us -> 33.1 us
    psum x11 -> x0, blocking collectives: 190 us -> none  [total_of(): x = lax.psum(x, axis)]
    ppermute x0 -> x30, starting transfers between devices: none -> 104 us  [total_of(): x = x + lax.ppermute(x, axis, [(i, i ^ step) for i in range(size)])]
    ppermute x0 -> x30, waiting for transfers between devices: none -> 39.5 us  [total_of(): x = x + lax.ppermute(x, axis, [(i, i ^ step) for i in range(size)])]
    all_to_all x1 -> x0, blocking collectives: 14.7 us -> none  [local(): out = lax.all_to_all(sparse, 'ba', 0, 1, tiled=True)]
    reduce_scatter x1, waiting for transfers between devices: 4.06 us -> 16.3 us  [local(): lax.psum_scatter(partial_grad, 'ba', scatter_dimension=0, tiled=True)]
    all_to_all x1, waiting for transfers between devices: 6.07 us -> 0.01 us  [local(): field = lax.all_to_all(abundance, 'ba', 1, 0, tiled=True)]
    all_to_all x0 -> x1, starting transfers between devices: none -> 5.96 us  [local(): out = lax.all_to_all(sparse, 'ba', 0, 1, tiled=True)]
    ppermute x6, waiting for transfers between devices: 13.5 us -> 18.7 us  [extended_2(): after = lax.ppermute(leading, axis, down)]
  transfers between devices with their start and end apart: 15 -> 46, of which waited for: 9 -> 38; matrix products, arithmetic and copies ran while one was open for 2% -> 4% of each run, Pallas kernels for 0% -> 0%
where the time goes in v2:
time: 299 us; the launch traced here: 296 us
  starting transfers between devices  146 us (49%)
  waiting for transfers between devices  74.7 us (25%)
  between operations  33.1 us (11%)
  blocking collectives  13.8 us (5%)
  matrix products  11.1 us (4%)
  local copies, waits for them, and re-layouts  9.1 us (3%)
  other arithmetic  8.27 us (3%)
    ppermute x30, starting transfers between devices, total_of(): x = x + lax.ppermute(x, axis, [(i, i ^ step) for i in range(size)])  104 us
    ppermute x30, waiting for transfers between devices, total_of(): x = x + lax.ppermute(x, axis, [(i, i ^ step) for i in range(size)])  39.5 us
    ppermute x6, waiting for transfers between devices, extended_2(): after = lax.ppermute(leading, axis, down)  18.7 us
    reduce_scatter x1, waiting for transfers between devices, local(): lax.psum_scatter(partial_grad, 'ba', scatter_dimension=0, tiled=True)  16.3 us
    ppermute x6, starting transfers between devices, extended_2(): before = lax.ppermute(last, axis, up)  15.2 us
    all_gather x1, blocking collectives, local(): all_spectra = lax.all_gather(spectra, 'ba', axis=0, tiled=True)  13.8 us
    ppermute x6, starting transfers between devices, extended_2(): after = lax.ppermute(leading, axis, down)  10.2 us
    unnamed x21, local copies, waits for them, and re-layouts  7.18 us
  transfers between devices with their start and end apart: 46, of which 38 were waited for; matrix products, arithmetic and copies ran while one was open for 4% of the time, Pallas kernels for 0%

profile of v2, /device:TPU:2, one launch (start us, length us, event | category | flops | bytes accessed | tf_op | source)
XLA Modules:
  0.0 296.1 jit_solution(1335524386169584928)
XLA Ops:
  9.2 5.8 %all-to-all-start = ((f32[64,16,128]{2,0,1:T(8,128)}), f32[64,16,128]{2,0,1:T(8,128)S(1)}, u32[]{:S(2)}, u32[]{:S(2)}) async-start(f32[64,16,128]{2,0,1:T(8,128)} %copy.35), calls=%async_computation | async-start | bytes 1048576 | tf_op jit(solution)/shard_map/all_to_all | solution.py:57
  15.0 13.8 %all_gather.3 = f32[224,256]{1,0:T(8,128)S(1)} all-gather(f32[56,256]{1,0:T(8,128)S(1)} %copy-done.7), channel_id=1, replica_groups=mesh['gx'=8,'gy'=8,'ba'=4] {'ba'}, dimensions={0}, use_global_device_ids=true | all-gather | bytes 286720 | tf_op jit(solution)/shard_map/all_gather | solution.py:64
  29.9 4.5 %all-to-all-start.1 = ((f32[56,16,128]{2,0,1:T(8,128)}), f32[56,16,128]{2,0,1:T(8,128)S(1)}, u32[]{:S(2)}, u32[]{:S(2)}) async-start(f32[56,16,128]{2,0,1:T(8,128)} %copy.37), calls=%async_computation.1 | async-start | bytes 917504 | tf_op jit(solution)/shard_map/all_to_all | solution.py:58
  42.1 3.4 %collective-permute-start.2 = (f32[256,1,130]{0,2,1:T(8,128)S(1)}, f32[256,1,130]{0,2,1:T(8,128)S(1)}, u32[]{:S(2)}, u32[]{:S(2)}) collective-permute-start(f32[256,1,130]{0,2,1:T(8,128)S(1)} %get-tuple-element.25), channel_id=1, source_target_pairs={{0,1},{1,2},{2,3},{3,4},{4,5},{5,6},{6,7},{7,8},{8,9},{9,10},{10,1... | collective-permute-start | bytes 399368 | tf_op jit(solution)/shard_map/ppermute | solution.py:26
  49.4 3.4 %collective-permute-done.3 = f32[256,1,130]{0,2,1:T(8,128)S(1)} collective-permute-done((f32[256,1,130]{0,2,1:T(8,128)S(1)}, f32[256,1,130]{0,2,1:T(8,128)S(1)}, u32[]{:S(2)}, u32[]{:S(2)}) %collective-permute-start.3) | collective-permute-done | bytes 133152 | tf_op jit(solution)/shard_map/ppermute | solution.py:27
  58.8 6.7 %collective-permute-start.5 = (f32[]{:T(128)}, f32[]{:T(128)}, u32[]{:S(2)}, u32[]{:S(2)}) collective-permute-start(f32[]{:T(128)} %add.254), channel_id=1, source_target_pairs={{0,2},{1,3},{2,0},{3,1},{4,6},{5,7},{6,4},{7,5},{8,10},{9,11},{10,... | collective-permute-start | bytes 20 | tf_op jit(solution)/shard_map/ppermute | solution.py:49
  66.4 3.3 %collective-permute-start.6 = (f32[]{:T(128)}, f32[]{:T(128)}, u32[]{:S(2)}, u32[]{:S(2)}) collective-permute-start(f32[]{:T(128)} %add.255), channel_id=1, source_target_pairs={{0,4},{4,0},{8,12},{12,8},{16,20},{20,16},{24,28},{28,24},{1,5},{5... | collective-permute-start | bytes 20 | tf_op jit(solution)/shard_map/ppermute | solution.py:49
  70.7 7.0 %collective-permute-start.7 = (f32[]{:T(128)}, f32[]{:T(128)}, u32[]{:S(2)}, u32[]{:S(2)}) collective-permute-start(f32[]{:T(128)} %add.256), channel_id=1, source_target_pairs={{0,8},{4,12},{8,0},{12,4},{16,24},{20,28},{24,16},{28,20},{1,9},{5... | collective-permute-start | bytes 20 | tf_op jit(solution)/shard_map/ppermute | solution.py:49
  78.5 5.0 %collective-permute-start.8 = (f32[]{:T(128)}, f32[]{:T(128)}, u32[]{:S(2)}, u32[]{:S(2)}) collective-permute-start(f32[]{:T(128)} %add.257), channel_id=1, source_target_pairs={{0,16},{4,20},{8,24},{12,28},{16,0},{20,4},{24,8},{28,12},{1,17},{... | collective-permute-start | bytes 20 | tf_op jit(solution)/shard_map/ppermute | solution.py:49
  88.6 4.1 %collective-permute-start.10 = (f32[]{:T(128)}, f32[]{:T(128)}, u32[]{:S(2)}, u32[]{:S(2)}) collective-permute-start(f32[]{:T(128)} %add.259), channel_id=1, source_target_pairs={{0,64},{32,96},{64,0},{96,32},{128,192},{160,224},{192,128},{224,1... | collective-permute-start | bytes 20 | tf_op jit(solution)/shard_map/ppermute | solution.py:49
  93.6 4.7 %collective-permute-start.11 = (f32[]{:T(128)}, f32[]{:T(128)}, u32[]{:S(2)}, u32[]{:S(2)}) collective-permute-start(f32[]{:T(128)} %add.260), channel_id=1, source_target_pairs={{0,128},{32,160},{64,192},{96,224},{128,0},{160,32},{192,64},{224,... | collective-permute-start | bytes 20 | tf_op jit(solution)/shard_map/ppermute | solution.py:49
  104.9 3.5 %collective-permute-done.13 = f32[256,4,1]{0,2,1:T(1,128)S(1)} collective-permute-done((f32[256,4,1]{0,2,1:T(1,128)S(1)}, f32[256,4,1]{0,2,1:T(1,128)S(1)}, u32[]{:S(2)}, u32[]{:S(2)}) %collective-permute-start.13) | collective-permute-done | bytes 4128 | tf_op jit(solution)/shard_map/ppermute | solution.py:27
  108.4 4.0 %collective-permute-start.14 = (f32[256,1,130]{0,2,1:T(8,128)S(1)}, f32[256,1,130]{0,2,1:T(8,128)S(1)}, u32[]{:S(2)}, u32[]{:S(2)}) collective-permute-start(f32[256,1,130]{0,2,1:T(8,128)S(1)} %get-tuple-element.23), channel_id=1, source_target_pairs={{0,1},{1,2},{2,3},{3,4},{4,5},{5,6},{6,7},{7,8},{8,9},{9,10},{10,1... | collective-permute-start | bytes 399368 | tf_op jit(solution)/shard_map/ppermute | solution.py:26
  115.8 3.6 %collective-permute-done.15 = f32[256,1,130]{0,2,1:T(8,128)S(1)} collective-permute-done((f32[256,1,130]{0,2,1:T(8,128)S(1)}, f32[256,1,130]{0,2,1:T(8,128)S(1)}, u32[]{:S(2)}, u32[]{:S(2)}) %collective-permute-start.15) | collective-permute-done | bytes 133152 | tf_op jit(solution)/shard_map/ppermute | solution.py:27
  120.5 3.8 %collective-permute-done.16 = f32[]{:T(128)} collective-permute-done((f32[]{:T(128)}, f32[]{:T(128)}, u32[]{:S(2)}, u32[]{:S(2)}) %collective-permute-start.16) | collective-permute-done | bytes 36 | tf_op jit(solution)/shard_map/ppermute | solution.py:49
  125.5 5.8 %collective-permute-start.17 = (f32[]{:T(128)}, f32[]{:T(128)}, u32[]{:S(2)}, u32[]{:S(2)}) collective-permute-start(f32[]{:T(128)} %add.275), channel_id=1, source_target_pairs={{0,2},{1,3},{2,0},{3,1},{4,6},{5,7},{6,4},{7,5},{8,10},{9,11},{10,... | collective-permute-start | bytes 20 | tf_op jit(solution)/shard_map/ppermute | solution.py:49
  136.7 4.6 %collective-permute-start.19 = (f32[]{:T(128)}, f32[]{:T(128)}, u32[]{:S(2)}, u32[]{:S(2)}) collective-permute-start(f32[]{:T(128)} %add.277), channel_id=1, source_target_pairs={{0,8},{4,12},{8,0},{12,4},{16,24},{20,28},{24,16},{28,20},{1,9},{5... | collective-permute-start | bytes 20 | tf_op jit(solution)/shard_map/ppermute | solution.py:49
  142.2 4.7 %collective-permute-start.20 = (f32[]{:T(128)}, f32[]{:T(128)}, u32[]{:S(2)}, u32[]{:S(2)}) collective-permute-start(f32[]{:T(128)} %add.278), channel_id=1, source_target_pairs={{0,16},{4,20},{8,24},{12,28},{16,0},{20,4},{24,8},{28,12},{1,17},{... | collective-permute-start | bytes 20 | tf_op jit(solution)/shard_map/ppermute | solution.py:49
  152.4 4.7 %collective-permute-start.22 = (f32[]{:T(128)}, f32[]{:T(128)}, u32[]{:S(2)}, u32[]{:S(2)}) collective-permute-start(f32[]{:T(128)} %add.280), channel_id=1, source_target_pairs={{0,64},{32,96},{64,0},{96,32},{128,192},{160,224},{192,128},{224,1... | collective-permute-start | bytes 20 | tf_op jit(solution)/shard_map/ppermute | solution.py:49
  158.0 5.1 %collective-permute-start.23 = (f32[]{:T(128)}, f32[]{:T(128)}, u32[]{:S(2)}, u32[]{:S(2)}) collective-permute-start(f32[]{:T(128)} %add.281), channel_id=1, source_target_pairs={{0,128},{32,160},{64,192},{96,224},{128,0},{160,32},{192,64},{224,... | collective-permute-start | bytes 20 | tf_op jit(solution)/shard_map/ppermute | solution.py:49
  170.1 3.3 %collective-permute-done.25 = f32[256,4,1]{0,2,1:T(1,128)S(1)} collective-permute-done((f32[256,4,1]{0,2,1:T(1,128)S(1)}, f32[256,4,1]{0,2,1:T(1,128)S(1)}, u32[]{:S(2)}, u32[]{:S(2)}) %collective-permute-start.25) | collective-permute-done | bytes 4128 | tf_op jit(solution)/shard_map/ppermute | solution.py:27
  173.5 4.0 %collective-permute-start.26 = (f32[256,1,130]{0,2,1:T(8,128)S(1)}, f32[256,1,130]{0,2,1:T(8,128)S(1)}, u32[]{:S(2)}, u32[]{:S(2)}) collective-permute-start(f32[256,1,130]{0,2,1:T(8,128)S(1)} %get-tuple-element.21), channel_id=1, source_target_pairs={{0,1},{1,2},{2,3},{3,4},{4,5},{5,6},{6,7},{7,8},{8,9},{9,10},{10,1... | collective-permute-start | bytes 399368 | tf_op jit(solution)/shard_map/ppermute | solution.py:26
  180.9 3.6 %collective-permute-done.27 = f32[256,1,130]{0,2,1:T(8,128)S(1)} collective-permute-done((f32[256,1,130]{0,2,1:T(8,128)S(1)}, f32[256,1,130]{0,2,1:T(8,128)S(1)}, u32[]{:S(2)}, u32[]{:S(2)}) %collective-permute-start.27) | collective-permute-done | bytes 133152 | tf_op jit(solution)/shard_map/ppermute | solution.py:27
  186.4 3.8 %collective-permute-done.28 = f32[]{:T(128)} collective-permute-done((f32[]{:T(128)}, f32[]{:T(128)}, u32[]{:S(2)}, u32[]{:S(2)}) %collective-permute-start.28) | collective-permute-done | bytes 36 | tf_op jit(solution)/shard_map/ppermute | solution.py:49
  191.4 5.8 %collective-permute-start.29 = (f32[]{:T(128)}, f32[]{:T(128)}, u32[]{:S(2)}, u32[]{:S(2)}) collective-permute-start(f32[]{:T(128)} %add.295), channel_id=1, source_target_pairs={{0,2},{1,3},{2,0},{3,1},{4,6},{5,7},{6,4},{7,5},{8,10},{9,11},{10,... | collective-permute-start | bytes 20 | tf_op jit(solution)/shard_map/ppermute | solution.py:49
  202.5 4.6 %collective-permute-start.31 = (f32[]{:T(128)}, f32[]{:T(128)}, u32[]{:S(2)}, u32[]{:S(2)}) collective-permute-start(f32[]{:T(128)} %add.297), channel_id=1, source_target_pairs={{0,8},{4,12},{8,0},{12,4},{16,24},{20,28},{24,16},{28,20},{1,9},{5... | collective-permute-start | bytes 20 | tf_op jit(solution)/shard_map/ppermute | solution.py:49
  208.0 4.7 %collective-permute-start.32 = (f32[]{:T(128)}, f32[]{:T(128)}, u32[]{:S(2)}, u32[]{:S(2)}) collective-permute-start(f32[]{:T(128)} %add.298), channel_id=1, source_target_pairs={{0,16},{4,20},{8,24},{12,28},{16,0},{20,4},{24,8},{28,12},{1,17},{... | collective-permute-start | bytes 20 | tf_op jit(solution)/shard_map/ppermute | solution.py:49
  218.2 4.3 %collective-permute-start.34 = (f32[]{:T(128)}, f32[]{:T(128)}, u32[]{:S(2)}, u32[]{:S(2)}) collective-permute-start(f32[]{:T(128)} %add.300), channel_id=1, source_target_pairs={{0,64},{32,96},{64,0},{96,32},{128,192},{160,224},{192,128},{224,1... | collective-permute-start | bytes 20 | tf_op jit(solution)/shard_map/ppermute | solution.py:49
  223.5 5.2 %collective-permute-start.35 = (f32[]{:T(128)}, f32[]{:T(128)}, u32[]{:S(2)}, u32[]{:S(2)}) collective-permute-start(f32[]{:T(128)} %add.301), channel_id=1, source_target_pairs={{0,128},{32,160},{64,192},{96,224},{128,0},{160,32},{192,64},{224,... | collective-permute-start | bytes 20 | tf_op jit(solution)/shard_map/ppermute | solution.py:49
  236.4 6.0 %all-to-all-start.2 = ((f32[256,4,128]{2,1,0:T(4,128)}), f32[256,4,128]{2,1,0:T(4,128)S(1)}, u32[]{:S(2)}, u32[]{:S(2)}) async-start(f32[256,4,128]{2,1,0:T(4,128)} %copy.47), calls=%async_computation.2 | async-start | bytes 1048576 | tf_op jit(solution)/shard_map/all_to_all | solution.py:102
  242.4 16.3 %reduce-scatter.2.cloned.1.call-done = f32[56,256]{1,0:T(8,128)} async-done(((f32[224,256]{1,0:T(8,128)}), f32[56,256]{1,0:T(8,128)}) %reduce-scatter.2.cloned.1.call-update) | async-done | bytes 57360 | tf_op jit(solution)/shard_map/reduce_scatter | solution.py:100
  280.5 5.7 %collective-permute-start.41 = (f32[56,256]{1,0:T(8,128)S(1)}, f32[56,256]{1,0:T(8,128)S(1)}, u32[]{:S(2)}, u32[]{:S(2)}) collective-permute-start(f32[56,256]{1,0:T(8,128)S(1)} %add.320), channel_id=1, source_target_pairs={{0,16},{4,20},{8,24},{12,28},{16,0},{20,4},{24,8},{28,12},{1,17},{... | collective-permute-start | bytes 172040 | tf_op jit(solution)/shard_map/ppermute | solution.py:49
  (130 shorter events, 94.4 us)
Async XLA Ops:
  9.2 20.7 %all-to-all-start = ((f32[64,16,128]{2,0,1:T(8,128)}), f32[64,16,128]{2,0,1:T(8,128)S(1)}, u32[]{:S(2)}, u32[]{:S(2)}) async-start(f32[64,16,128]{2,0,1:T(8,128)} %copy.35), calls=%async_computation | async-start | bytes 1048576 | tf_op jit(solution)/shard_map/all_to_all | solution.py:57
  29.9 10.8 %all-to-all-start.1 = ((f32[56,16,128]{2,0,1:T(8,128)}), f32[56,16,128]{2,0,1:T(8,128)S(1)}, u32[]{:S(2)}, u32[]{:S(2)}) async-start(f32[56,16,128]{2,0,1:T(8,128)} %copy.37), calls=%async_computation.1 | async-start | bytes 917504 | tf_op jit(solution)/shard_map/all_to_all | solution.py:58
  34.4 224.3 %reduce-scatter.2.cloned.1.call-start = ((), (), s32[]{:S(2)}) async-start(), calls=%async_computation.4 | async-start | bytes 286720 | tf_op jit(solution)/shard_map/reduce_scatter | solution.py:100
  35.3 5.3 %collective-permute-start = (f32[256,4,1]{0,2,1:T(1,128)S(1)}, f32[256,4,1]{0,2,1:T(1,128)S(1)}, u32[]{:S(2)}, u32[]{:S(2)}) collective-permute-start(f32[256,4,1]{0,2,1:T(1,128)S(1)} %get-tuple-element.30), channel_id=1, source_target_pairs={{0,32},{32,64},{64,96},{96,128},{128,160},{160,192},{192,224},{1,3... | collective-permute-start | bytes 12296 | tf_op jit(solution)/shard_map/ppermute | solution.py:26
  36.6 5.4 %collective-permute-start.1 = (f32[256,4,1]{0,2,1:T(1,128)S(1)}, f32[256,4,1]{0,2,1:T(1,128)S(1)}, u32[]{:S(2)}, u32[]{:S(2)}) collective-permute-start(f32[256,4,1]{0,2,1:T(1,128)S(1)} %get-tuple-element.31), channel_id=1, source_target_pairs={{32,0},{64,32},{96,64},{128,96},{160,128},{192,160},{224,192},{33,... | collective-permute-start | bytes 12296 | tf_op jit(solution)/shard_map/ppermute | solution.py:27
  42.1 7.2 %collective-permute-start.2 = (f32[256,1,130]{0,2,1:T(8,128)S(1)}, f32[256,1,130]{0,2,1:T(8,128)S(1)}, u32[]{:S(2)}, u32[]{:S(2)}) collective-permute-start(f32[256,1,130]{0,2,1:T(8,128)S(1)} %get-tuple-element.25), channel_id=1, source_target_pairs={{0,1},{1,2},{2,3},{3,4},{4,5},{5,6},{6,7},{7,8},{8,9},{9,10},{10,1... | collective-permute-start | bytes 399368 | tf_op jit(solution)/shard_map/ppermute | solution.py:26
  45.5 7.3 %collective-permute-start.3 = (f32[256,1,130]{0,2,1:T(8,128)S(1)}, f32[256,1,130]{0,2,1:T(8,128)S(1)}, u32[]{:S(2)}, u32[]{:S(2)}) collective-permute-start(f32[256,1,130]{0,2,1:T(8,128)S(1)} %get-tuple-element.24), channel_id=1, source_target_pairs={{1,0},{2,1},{3,2},{4,3},{5,4},{6,5},{7,6},{8,7},{9,8},{10,9},{11,1... | collective-permute-start | bytes 399368 | tf_op jit(solution)/shard_map/ppermute | solution.py:27
  58.8 6.9 %collective-permute-start.5 = (f32[]{:T(128)}, f32[]{:T(128)}, u32[]{:S(2)}, u32[]{:S(2)}) collective-permute-start(f32[]{:T(128)} %add.254), channel_id=1, source_target_pairs={{0,2},{1,3},{2,0},{3,1},{4,6},{5,7},{6,4},{7,5},{8,10},{9,11},{10,... | collective-permute-start | bytes 20 | tf_op jit(solution)/shard_map/ppermute | solution.py:49
  70.7 7.2 %collective-permute-start.7 = (f32[]{:T(128)}, f32[]{:T(128)}, u32[]{:S(2)}, u32[]{:S(2)}) collective-permute-start(f32[]{:T(128)} %add.256), channel_id=1, source_target_pairs={{0,8},{4,12},{8,0},{12,4},{16,24},{20,28},{24,16},{28,20},{1,9},{5... | collective-permute-start | bytes 20 | tf_op jit(solution)/shard_map/ppermute | solution.py:49
  78.5 7.5 %collective-permute-start.8 = (f32[]{:T(128)}, f32[]{:T(128)}, u32[]{:S(2)}, u32[]{:S(2)}) collective-permute-start(f32[]{:T(128)} %add.257), channel_id=1, source_target_pairs={{0,16},{4,20},{8,24},{12,28},{16,0},{20,4},{24,8},{28,12},{1,17},{... | collective-permute-start | bytes 20 | tf_op jit(solution)/shard_map/ppermute | solution.py:49
  93.6 5.1 %collective-permute-start.11 = (f32[]{:T(128)}, f32[]{:T(128)}, u32[]{:S(2)}, u32[]{:S(2)}) collective-permute-start(f32[]{:T(128)} %add.260), channel_id=1, source_target_pairs={{0,128},{32,160},{64,192},{96,224},{128,0},{160,32},{192,64},{224,... | collective-permute-start | bytes 20 | tf_op jit(solution)/shard_map/ppermute | solution.py:49
  103.0 5.3 %collective-permute-start.13 = (f32[256,4,1]{0,2,1:T(1,128)S(1)}, f32[256,4,1]{0,2,1:T(1,128)S(1)}, u32[]{:S(2)}, u32[]{:S(2)}) collective-permute-start(f32[256,4,1]{0,2,1:T(1,128)S(1)} %get-tuple-element.29), channel_id=1, source_target_pairs={{32,0},{64,32},{96,64},{128,96},{160,128},{192,160},{224,192},{33,... | collective-permute-start | bytes 12296 | tf_op jit(solution)/shard_map/ppermute | solution.py:27
  108.4 7.4 %collective-permute-start.14 = (f32[256,1,130]{0,2,1:T(8,128)S(1)}, f32[256,1,130]{0,2,1:T(8,128)S(1)}, u32[]{:S(2)}, u32[]{:S(2)}) collective-permute-start(f32[256,1,130]{0,2,1:T(8,128)S(1)} %get-tuple-element.23), channel_id=1, source_target_pairs={{0,1},{1,2},{2,3},{3,4},{4,5},{5,6},{6,7},{7,8},{8,9},{9,10},{10,1... | collective-permute-start | bytes 399368 | tf_op jit(solution)/shard_map/ppermute | solution.py:26
  112.4 7.1 %collective-permute-start.15 = (f32[256,1,130]{0,2,1:T(8,128)S(1)}, f32[256,1,130]{0,2,1:T(8,128)S(1)}, u32[]{:S(2)}, u32[]{:S(2)}) collective-permute-start(f32[256,1,130]{0,2,1:T(8,128)S(1)} %get-tuple-element.22), channel_id=1, source_target_pairs={{1,0},{2,1},{3,2},{4,3},{5,4},{6,5},{7,6},{8,7},{9,8},{10,9},{11,1... | collective-permute-start | bytes 399368 | tf_op jit(solution)/shard_map/ppermute | solution.py:27
  125.5 6.2 %collective-permute-start.17 = (f32[]{:T(128)}, f32[]{:T(128)}, u32[]{:S(2)}, u32[]{:S(2)}) collective-permute-start(f32[]{:T(128)} %add.275), channel_id=1, source_target_pairs={{0,2},{1,3},{2,0},{3,1},{4,6},{5,7},{6,4},{7,5},{8,10},{9,11},{10,... | collective-permute-start | bytes 20 | tf_op jit(solution)/shard_map/ppermute | solution.py:49
  136.7 5.0 %collective-permute-start.19 = (f32[]{:T(128)}, f32[]{:T(128)}, u32[]{:S(2)}, u32[]{:S(2)}) collective-permute-start(f32[]{:T(128)} %add.277), channel_id=1, source_target_pairs={{0,8},{4,12},{8,0},{12,4},{16,24},{20,28},{24,16},{28,20},{1,9},{5... | collective-permute-start | bytes 20 | tf_op jit(solution)/shard_map/ppermute | solution.py:49
  142.2 7.7 %collective-permute-start.20 = (f32[]{:T(128)}, f32[]{:T(128)}, u32[]{:S(2)}, u32[]{:S(2)}) collective-permute-start(f32[]{:T(128)} %add.278), channel_id=1, source_target_pairs={{0,16},{4,20},{8,24},{12,28},{16,0},{20,4},{24,8},{28,12},{1,17},{... | collective-permute-start | bytes 20 | tf_op jit(solution)/shard_map/ppermute | solution.py:49
  152.4 5.0 %collective-permute-start.22 = (f32[]{:T(128)}, f32[]{:T(128)}, u32[]{:S(2)}, u32[]{:S(2)}) collective-permute-start(f32[]{:T(128)} %add.280), channel_id=1, source_target_pairs={{0,64},{32,96},{64,0},{96,32},{128,192},{160,224},{192,128},{224,1... | collective-permute-start | bytes 20 | tf_op jit(solution)/shard_map/ppermute | solution.py:49
  158.0 5.4 %collective-permute-start.23 = (f32[]{:T(128)}, f32[]{:T(128)}, u32[]{:S(2)}, u32[]{:S(2)}) collective-permute-start(f32[]{:T(128)} %add.281), channel_id=1, source_target_pairs={{0,128},{32,160},{64,192},{96,224},{128,0},{160,32},{192,64},{224,... | collective-permute-start | bytes 20 | tf_op jit(solution)/shard_map/ppermute | solution.py:49
  168.3 5.1 %collective-permute-start.25 = (f32[256,4,1]{0,2,1:T(1,128)S(1)}, f32[256,4,1]{0,2,1:T(1,128)S(1)}, u32[]{:S(2)}, u32[]{:S(2)}) collective-permute-start(f32[256,4,1]{0,2,1:T(1,128)S(1)} %get-tuple-element.27), channel_id=1, source_target_pairs={{32,0},{64,32},{96,64},{128,96},{160,128},{192,160},{224,192},{33,... | collective-permute-start | bytes 12296 | tf_op jit(solution)/shard_map/ppermute | solution.py:27
  173.5 7.4 %collective-permute-start.26 = (f32[256,1,130]{0,2,1:T(8,128)S(1)}, f32[256,1,130]{0,2,1:T(8,128)S(1)}, u32[]{:S(2)}, u32[]{:S(2)}) collective-permute-start(f32[256,1,130]{0,2,1:T(8,128)S(1)} %get-tuple-element.21), channel_id=1, source_target_pairs={{0,1},{1,2},{2,3},{3,4},{4,5},{5,6},{6,7},{7,8},{8,9},{9,10},{10,1... | collective-permute-start | bytes 399368 | tf_op jit(solution)/shard_map/ppermute | solution.py:26
  177.4 7.1 %collective-permute-start.27 = (f32[256,1,130]{0,2,1:T(8,128)S(1)}, f32[256,1,130]{0,2,1:T(8,128)S(1)}, u32[]{:S(2)}, u32[]{:S(2)}) collective-permute-start(f32[256,1,130]{0,2,1:T(8,128)S(1)} %get-tuple-element.20), channel_id=1, source_target_pairs={{1,0},{2,1},{3,2},{4,3},{5,4},{6,5},{7,6},{8,7},{9,8},{10,9},{11,1... | collective-permute-start | bytes 399368 | tf_op jit(solution)/shard_map/ppermute | solution.py:27
  191.4 6.2 %collective-permute-start.29 = (f32[]{:T(128)}, f32[]{:T(128)}, u32[]{:S(2)}, u32[]{:S(2)}) collective-permute-start(f32[]{:T(128)} %add.295), channel_id=1, source_target_pairs={{0,2},{1,3},{2,0},{3,1},{4,6},{5,7},{6,4},{7,5},{8,10},{9,11},{10,... | collective-permute-start | bytes 20 | tf_op jit(solution)/shard_map/ppermute | solution.py:49
  202.5 5.0 %collective-permute-start.31 = (f32[]{:T(128)}, f32[]{:T(128)}, u32[]{:S(2)}, u32[]{:S(2)}) collective-permute-start(f32[]{:T(128)} %add.297), channel_id=1, source_target_pairs={{0,8},{4,12},{8,0},{12,4},{16,24},{20,28},{24,16},{28,20},{1,9},{5... | collective-permute-start | bytes 20 | tf_op jit(solution)/shard_map/ppermute | solution.py:49
  208.0 7.7 %collective-permute-start.32 = (f32[]{:T(128)}, f32[]{:T(128)}, u32[]{:S(2)}, u32[]{:S(2)}) collective-permute-start(f32[]{:T(128)} %add.298), channel_id=1, source_target_pairs={{0,16},{4,20},{8,24},{12,28},{16,0},{20,4},{24,8},{28,12},{1,17},{... | collective-permute-start | bytes 20 | tf_op jit(solution)/shard_map/ppermute | solution.py:49
  218.2 4.7 %collective-permute-start.34 = (f32[]{:T(128)}, f32[]{:T(128)}, u32[]{:S(2)}, u32[]{:S(2)}) collective-permute-start(f32[]{:T(128)} %add.300), channel_id=1, source_target_pairs={{0,64},{32,96},{64,0},{96,32},{128,192},{160,224},{192,128},{224,1... | collective-permute-start | bytes 20 | tf_op jit(solution)/shard_map/ppermute | solution.py:49
  223.5 5.5 %collective-permute-start.35 = (f32[]{:T(128)}, f32[]{:T(128)}, u32[]{:S(2)}, u32[]{:S(2)}) collective-permute-start(f32[]{:T(128)} %add.301), channel_id=1, source_target_pairs={{0,128},{32,160},{64,192},{96,224},{128,0},{160,32},{192,64},{224,... | collective-permute-start | bytes 20 | tf_op jit(solution)/shard_map/ppermute | solution.py:49
  236.4 49.8 %all-to-all-start.2 = ((f32[256,4,128]{2,1,0:T(4,128)}), f32[256,4,128]{2,1,0:T(4,128)S(1)}, u32[]{:S(2)}, u32[]{:S(2)}) async-start(f32[256,4,128]{2,1,0:T(4,128)} %copy.47), calls=%async_computation.2 | async-start | bytes 1048576 | tf_op jit(solution)/shard_map/all_to_all | solution.py:102
  265.1 5.8 %collective-permute-start.38 = (f32[56,256]{1,0:T(8,128)S(1)}, f32[56,256]{1,0:T(8,128)S(1)}, u32[]{:S(2)}, u32[]{:S(2)}) collective-permute-start(f32[56,256]{1,0:T(8,128)S(1)} %add.317), channel_id=1, source_target_pairs={{0,128},{32,160},{64,192},{96,224},{128,0},{160,32},{192,64},{224,... | collective-permute-start | bytes 172040 | tf_op jit(solution)/shard_map/ppermute | solution.py:49
  270.9 4.3 %collective-permute-start.39 = (f32[56,256]{1,0:T(8,128)S(1)}, f32[56,256]{1,0:T(8,128)S(1)}, u32[]{:S(2)}, u32[]{:S(2)}) collective-permute-start(f32[56,256]{1,0:T(8,128)S(1)} %add.318), channel_id=1, source_target_pairs={{0,4},{4,0},{8,12},{12,8},{16,20},{20,16},{24,28},{28,24},{1,5},{5... | collective-permute-start | bytes 172040 | tf_op jit(solution)/shard_map/ppermute | solution.py:49
  275.2 5.3 %collective-permute-start.40 = (f32[56,256]{1,0:T(8,128)S(1)}, f32[56,256]{1,0:T(8,128)S(1)}, u32[]{:S(2)}, u32[]{:S(2)}) collective-permute-start(f32[56,256]{1,0:T(8,128)S(1)} %add.319), channel_id=1, source_target_pairs={{0,8},{4,12},{8,0},{12,4},{16,24},{20,28},{24,16},{28,20},{1,9},{5... | collective-permute-start | bytes 172040 | tf_op jit(solution)/shard_map/ppermute | solution.py:49
  280.5 8.2 %collective-permute-start.41 = (f32[56,256]{1,0:T(8,128)S(1)}, f32[56,256]{1,0:T(8,128)S(1)}, u32[]{:S(2)}, u32[]{:S(2)}) collective-permute-start(f32[56,256]{1,0:T(8,128)S(1)} %add.320), channel_id=1, source_target_pairs={{0,16},{4,20},{8,24},{12,28},{16,0},{20,4},{24,8},{28,12},{1,17},{... | collective-permute-start | bytes 172040 | tf_op jit(solution)/shard_map/ppermute | solution.py:49
  (23 other events, 120.9 us)
Sparse Core Ops, SparseCore 0:
  235.5 23.0 reduce-scatter.1
